TPU v7x, 32 devices: a whole 2x2x4 slice. The times are simulated.
32 devices in a mesh: pulse: 16 (over z, x, core), range: 2 (over y).
Axes of the slice: x: 2, y: 2, z: 4, core: 2. Of those that a mesh axis runs over, the one named last changes fastest.
Arguments:
- echo: bfloat16 [32, 2, 32768], P('pulse', None, 'range'), may hold values from -6 to 6
- chirp_phase: float32 [256], replicated, may hold values from -0.5 to 201.5624
- rec_phase: float32 [2, 2048, 2], P('range', 'pulse'), may hold values from -3.140625 to 3.140625
- rec_start: int32 [2, 2048], P('range', 'pulse'), may hold values from 0 to 32256
- rec_owner: int32 [2, 2048, 1], P('range', 'pulse'), may hold values from 0 to 31; in each aligned block of 128 rows (0 to 127, 128 to 255, ..., all dimensions but the last counted through in order) at most 6 rows name the same one
- rec_row: int32 [2, 2048], P('range', 'pulse'), may hold values from 0 to 63
- rec_weight: float32 [2, 2048], P('range', 'pulse'), may hold values from 0.2 to 1
- rec_count: int32 [2, 16], P('range', 'pulse'), may hold values from 96 to 128, as said below
- prior: bfloat16 [512, 2, 1024], P('pulse', None, 'range'), may hold values from -6 to 6
- interp_weight: bfloat16 [64, 32], replicated, may hold values from -1 to 1
Outputs:
- tiles: float32 [1024, 2, 1024], P('pulse', None, 'range')
Inputs may be any that keep to these rules, and one draw needn't show every extreme that they name: `rec_owner`: in each aligned block of 128 record slots (one device's slots) no owner is named more than 6 times. Owner o is the tile of pulse index o // 2 and range index o % 2, 2 being the number of range devices. `rec_count`: some subimage has all 128 slots live.
All inputs are finite; a program needn't handle non-finite values.
Results may differ from a plain program's by a relative error of at most 0.0034.
Values may be sent and summed in bfloat16 or wider, within the bound.
No kernel may reach another device: no remote copies, remote signals or barrier semaphores. Data moves between devices by JAX's collectives and lax.ppermute only.
A program may use at most 64 MiB of HBM per device.

v0:
```python
import jax
import jax.numpy as jnp
from jax import lax
from jax.sharding import PartitionSpec as P

SEG = 512


def chirp_matrix(chirp_phase):
    tap_count = chirp_phase.shape[0]
    tap_scale = 1.0 / jnp.sqrt(jnp.float32(tap_count))
    real_taps = jnp.cos(chirp_phase) * tap_scale
    imag_taps = jnp.sin(chirp_phase) * tap_scale

    def banded(values):
        padded = jnp.concatenate([values, jnp.zeros((tap_count + 1,), jnp.float32)])
        return (
            jnp.tile(padded, tap_count)[: 2 * tap_count * tap_count]
            .reshape(tap_count, 2 * tap_count)
            .T
        )

    real_band = banded(real_taps)
    imag_band = banded(imag_taps)
    upper = jnp.concatenate([real_band, -imag_band], axis=1)
    lower = jnp.concatenate([imag_band, real_band], axis=1)
    return jnp.concatenate([upper, lower], axis=0).astype(jnp.bfloat16)


def compress(echo_block, tail_rim, filter_matrix):
    pulses, planes, bin_count = echo_block.shape
    tap_count = filter_matrix.shape[1] // 2
    block_count = bin_count // tap_count
    extended = jnp.concatenate([echo_block, tail_rim], axis=2)
    left_half = extended[:, :, :bin_count].reshape(pulses, planes, block_count, tap_count)
    right_half = extended[:, :, tap_count:].reshape(pulses, planes, block_count, tap_count)
    windows = jnp.concatenate([left_half, right_half], axis=3)
    windows = windows.transpose(0, 2, 1, 3).reshape(pulses * block_count, 2 * planes * tap_count)
    filtered = jnp.dot(windows, filter_matrix, preferred_element_type=jnp.float32)
    filtered = filtered.reshape(pulses, block_count, planes, tap_count).transpose(0, 2, 1, 3)
    return filtered.reshape(pulses, planes, bin_count).astype(jnp.bfloat16)


def cut_windows(block_table, starts):
    block_total = block_table.shape[0]
    first_block = starts // SEG
    second_block = jnp.minimum(first_block + 1, block_total - 1)
    offsets = starts % SEG
    paired = jnp.concatenate([block_table[first_block], block_table[second_block]], axis=3)
    for bit_number in range((SEG - 1).bit_length()):
        step_size = 1 << bit_number
        moved = jnp.concatenate(
            [paired[..., step_size:], jnp.zeros(paired.shape[:-1] + (step_size,), paired.dtype)],
            axis=3,
        )
        chosen = (offsets // step_size % 2 == 1)[:, None, None, None]
        paired = jnp.where(chosen, moved, paired)
    return paired[..., :SEG]


def form_records(block_table, starts, phases, scales):
    windows = cut_windows(block_table, starts)
    cosine = jnp.cos(phases).astype(jnp.bfloat16)
    sine_part = jnp.sin(phases).astype(jnp.bfloat16)
    real_part = windows[:, :, 0]
    imag_part = windows[:, :, 1]
    out_real = jnp.einsum(
        "bk,bks->bs", cosine, real_part, preferred_element_type=jnp.float32
    ) - jnp.einsum("bk,bks->bs", sine_part, imag_part, preferred_element_type=jnp.float32)
    out_imag = jnp.einsum(
        "bk,bks->bs", cosine, imag_part, preferred_element_type=jnp.float32
    ) + jnp.einsum("bk,bks->bs", sine_part, real_part, preferred_element_type=jnp.float32)
    return (jnp.stack([out_real, out_imag], axis=1) * scales[:, None, None]).astype(jnp.bfloat16)


def on_device(
    echo,
    chirp_phase,
    rec_phase,
    rec_start,
    rec_owner,
    rec_row,
    rec_weight,
    rec_count,
    prior,
    interp_weight,
):
    filter_matrix = chirp_matrix(chirp_phase)
    tap_count = chirp_phase.shape[0]
    raw_echo = lax.all_gather(echo, "range", axis=2, tiled=True)
    profiles = compress(raw_echo, jnp.zeros_like(raw_echo[:, :, :tap_count]), filter_matrix)
    pulses, planes, bin_total = profiles.shape
    block_table = profiles.reshape(pulses, planes, bin_total // SEG, SEG).transpose(2, 0, 1, 3)
    slot_count = rec_start.shape[1]
    starts = rec_start[0]
    phases = rec_phase[0]
    owners = rec_owner[0, :, 0]
    dest_rows = rec_row[0]
    weights = rec_weight[0]
    live_mask = (jnp.arange(slot_count) < rec_count[0, 0]).astype(jnp.float32)
    scales = live_mask * weights / jnp.sqrt(jnp.float32(pulses))
    block_size = min(64, slot_count)
    group_count = slot_count // block_size

    def form_group(items):
        return form_records(block_table, items[0], items[1], items[2])

    records = lax.map(
        form_group,
        (
            starts.reshape(group_count, block_size),
            phases.reshape(group_count, block_size, pulses),
            scales.reshape(group_count, block_size),
        ),
    )
    records = records.reshape(slot_count, 2 * SEG)
    pulse_count = lax.axis_size("pulse")
    range_count = lax.axis_size("range")
    owner_total = pulse_count * range_count
    capacity = max(2, 3 * slot_count // (2 * owner_total))
    owner_marks = (owners[:, None] == jnp.arange(owner_total)[None, :]).astype(jnp.int32)
    earlier = jnp.cumsum(owner_marks, axis=0) - owner_marks
    slot_rank = jnp.sum(earlier * owner_marks, axis=1)
    slot_index = owners * capacity + slot_rank
    placement = slot_index[None, :] == jnp.arange(owner_total * capacity)[:, None]
    outgoing = jnp.dot(
        placement.astype(jnp.bfloat16), records, preferred_element_type=jnp.float32
    ).astype(jnp.bfloat16)
    row_slots = jnp.sum(placement.astype(jnp.int32) * dest_rows[None, :], axis=1)
    outgoing = outgoing.reshape(pulse_count, range_count, capacity, 2, SEG)
    row_slots = row_slots.reshape(pulse_count, range_count, capacity)
    incoming, incoming_rows = (
        lax.all_to_all(
            lax.all_to_all(outgoing, "pulse", split_axis=0, concat_axis=0, tiled=True),
            "range",
            split_axis=1,
            concat_axis=1,
            tiled=True,
        ),
        lax.all_to_all(
            lax.all_to_all(row_slots, "pulse", split_axis=0, concat_axis=0, tiled=True),
            "range",
            split_axis=1,
            concat_axis=1,
            tiled=True,
        ),
    )
    incoming = incoming.reshape(-1, 2, SEG)
    incoming_rows = incoming_rows.reshape(-1)
    out_rows = interp_weight.shape[0]
    tile_image = jnp.einsum("rm,mcs->rcs", interp_weight, prior, preferred_element_type=jnp.float32)
    row_table = (incoming_rows[:, None] == jnp.arange(out_rows)[None, :]).astype(jnp.bfloat16)
    tile_image = tile_image + jnp.einsum(
        "jr,jcs->rcs", row_table, incoming, preferred_element_type=jnp.float32
    )
    return tile_image


def solution(mesh):
    placed = (
        P("pulse", None, "range"),
        P(),
        P("range", "pulse", None),
        P("range", "pulse"),
        P("range", "pulse", None),
        P("range", "pulse"),
        P("range", "pulse"),
        P("range", "pulse"),
        P("pulse", None, "range"),
        P(),
    )
    return jax.shard_map(
        on_device, mesh=mesh, in_specs=placed, out_specs=P("pulse", None, "range"), check_vma=False
    )
```

profile of v0, /device:TPU:0, one launch (start us, length us, event | category | flops | bytes accessed | tf_op | source)
XLA Modules:
  0.0 105.9 jit_solution(2789000673935303853)
XLA Ops:
  4.0 7.4 %all-to-all-start = ((s32[16,2,6]{2,1,0:T(2,128)}), s32[16,2,6]{2,1,0:T(2,128)S(1)}, u32[]{:S(2)}, u32[]{:S(2)}) async-start(s32[16,2,6]{2,1,0:T(2,128)} %reshape.452), calls=%async_computation | async-start | bytes 32768 | tf_op jit(solution)/shard_map/all_to_all | solution.py:141
  14.1 6.5 %all_gather.3 = bf16[2,2,32768]{2,1,0:T(2,128)(2,1)S(1)} all-gather(bf16[2,2,16384]{2,1,0:T(2,128)(2,1)S(1)} %copy-done.1), channel_id=1, replica_groups=mesh['pulse'=16,'range'=2] {'range'}, dimensions={2}, use_global_device_ids=true | all-gather | bytes 393216 | tf_op jit(solution)/shard_map/all_gather | solution.py:90
  26.1 42.6 %while.13 = (s32[]{:T(128)}, bf16[2,64,2,512]{3,2,1,0:T(2,128)(2,1)S(1)}, f32[2,64,2]{1,0,2:T(2,128)S(1)}, s32[2,64]{1,0:T(2,128)S(1)}, bf16[64,2,2,512]{3,2,1,0...) while((s32[]{:T(128)}, bf16[2,64,2,512]{3,2,1,0:T(2,128)(2,1)S(1)}, f32[2,64,2]{1,0,2:T(2,128)S(1)}, ...), condition=%wide.region_4.5_spmd, body=%wide.region_3.4_spmd.sunk | while | flops 3162434 | bytes 28723936 | solution.py:108
  26.3 1.1 %gather_fusion = bf16[64,2,2,512]{3,2,1,0:T(2,128)(2,1)S(1)} fusion(bf16[64,2,2,512]{3,2,1,0:T(2,128)(2,1)S(1)} %get-tuple-element.289, s32[1024]{0:T(1024)S(1)} %get-tuple-element.256), kind=kCustom, calls=%fused_computation.clone.1 | custom fusion | bytes 524544 | tf_op jit(solution)/shard_map/while/body/eval_jaxpr/gather | solution.py:49
  27.6 1.1 %gather_fusion.1 = bf16[64,2,2,512]{3,2,1,0:T(2,128)(2,1)S(1)} fusion(bf16[64,2,2,512]{3,2,1,0:T(2,128)(2,1)S(1)} %get-tuple-element.289, s32[1024]{0:T(1024)S(1)} %get-tuple-element.257), kind=kCustom, calls=%fused_computation.1.clone.1 | custom fusion | bytes 524544 | tf_op jit(solution)/shard_map/while/body/eval_jaxpr/gather | solution.py:49
  28.9 1.0 slice.134
  31.0 1.0 slice.135
  33.0 1.0 slice.136
  34.0 1.0 broadcast_select_fusion.20
  35.0 1.0 slice.137
  36.0 1.0 broadcast_select_fusion.21
  37.0 1.0 slice.138
  39.0 1.0 slice.139
  41.0 1.0 slice.140
  47.5 1.1 %gather_fusion = bf16[64,2,2,512]{3,2,1,0:T(2,128)(2,1)S(1)} fusion(bf16[64,2,2,512]{3,2,1,0:T(2,128)(2,1)S(1)} %get-tuple-element.289, s32[1024]{0:T(1024)S(1)} %get-tuple-element.256), kind=kCustom, calls=%fused_computation.clone.1 | custom fusion | bytes 524544 | tf_op jit(solution)/shard_map/while/body/eval_jaxpr/gather | solution.py:49
  48.8 1.1 %gather_fusion.1 = bf16[64,2,2,512]{3,2,1,0:T(2,128)(2,1)S(1)} fusion(bf16[64,2,2,512]{3,2,1,0:T(2,128)(2,1)S(1)} %get-tuple-element.289, s32[1024]{0:T(1024)S(1)} %get-tuple-element.257), kind=kCustom, calls=%fused_computation.1.clone.1 | custom fusion | bytes 524544 | tf_op jit(solution)/shard_map/while/body/eval_jaxpr/gather | solution.py:49
  50.2 1.0 slice.134
  52.2 1.0 slice.135
  54.2 1.0 slice.136
  56.2 1.0 slice.137
  58.2 1.0 slice.138
  60.2 1.0 slice.139
  62.2 1.0 slice.140
  63.2 1.0 broadcast_select_fusion.24
  69.0 1.0 reshape.458
  70.0 5.8 %all-to-all-start.2 = ((bf16[16,2,6,2,512]{4,3,2,1,0:T(2,128)(2,1)}), bf16[16,2,6,2,512]{4,3,2,1,0:T(2,128)(2,1)S(1)}, u32[]{:S(2)}, u32[]{:S(2)}) async-start(bf16[16,2,6,2,512]{4,3,2,1,0:T(2,128)(2,1)} %reshape.458), calls=%async_computation.2 | async-start | bytes 786432 | tf_op jit(solution)/shard_map/all_to_all | solution.py:134
  76.6 11.5 %all-to-all-done.2 = bf16[16,2,6,2,512]{4,3,2,1,0:T(2,128)(2,1)S(1)} async-done(((bf16[16,2,6,2,512]{4,3,2,1,0:T(2,128)(2,1)}), bf16[16,2,6,2,512]{4,3,2,1,0:T(2,128)(2,1)S(1)}, u32[]{:S(2)}, u32[]{:S(2)}) %all-to-all-start.2) | async-done | bytes 393248 | tf_op jit(solution)/shard_map/all_to_all | solution.py:134
  88.1 3.2 %all-to-all-start.1 = ((s32[16,2,6]{0,2,1:T(8,128)}), s32[16,2,6]{0,2,1:T(8,128)S(1)}, u32[]{:S(2)}, u32[]{:S(2)}) async-start(s32[16,2,6]{0,2,1:T(8,128)} %copy.62), calls=%async_computation.1 | async-start | bytes 16384 | tf_op jit(solution)/shard_map/all_to_all | solution.py:140
  91.3 1.0 copy.68
  92.3 2.8 %all-to-all-done.1 = s32[16,2,6]{0,2,1:T(8,128)S(1)} async-done(((s32[16,2,6]{0,2,1:T(8,128)}), s32[16,2,6]{0,2,1:T(8,128)S(1)}, u32[]{:S(2)}, u32[]{:S(2)}) %all-to-all-start.1) | async-done | bytes 800 | tf_op jit(solution)/shard_map/all_to_all | solution.py:140
  95.1 3.5 %all-to-all-start.3 = ((bf16[16,2,6,2,512]{4,3,2,0,1:T(2,128)(2,1)}), bf16[16,2,6,2,512]{4,3,2,0,1:T(2,128)(2,1)S(1)}, u32[]{:S(2)}, u32[]{:S(2)}) async-start(bf16[16,2,6,2,512]{4,3,2,0,1:T(2,128)(2,1)} %copy.68), calls=%async_computation.3 | async-start | bytes 786432 | tf_op jit(solution)/shard_map/all_to_all | solution.py:133
  99.0 5.5 %all-to-all-done.3 = bf16[16,2,6,2,512]{4,3,2,0,1:T(2,128)(2,1)S(1)} async-done(((bf16[16,2,6,2,512]{4,3,2,0,1:T(2,128)(2,1)}), bf16[16,2,6,2,512]{4,3,2,0,1:T(2,128)(2,1)S(1)}, u32[]{:S(2)}, u32[]{:S(2)}) %all-to-all-start.3) | async-done | bytes 393248 | tf_op jit(solution)/shard_map/all_to_all | solution.py:133
  (127 shorter events, 34.6 us)
Async XLA Ops:
  0.0 98.6 %copy-start = (bf16[32,2,512]{2,1,0:T(2,128)(2,1)S(1)}, bf16[32,2,512]{2,1,0:T(2,128)(2,1)}, u32[]{:S(2)}) copy-start(bf16[32,2,512]{2,1,0:T(2,128)(2,1)} %param.20) | copy-start | bytes 196612
  4.0 66.1 %all-to-all-start = ((s32[16,2,6]{2,1,0:T(2,128)}), s32[16,2,6]{2,1,0:T(2,128)S(1)}, u32[]{:S(2)}, u32[]{:S(2)}) async-start(s32[16,2,6]{2,1,0:T(2,128)} %reshape.452), calls=%async_computation | async-start | bytes 32768 | tf_op jit(solution)/shard_map/all_to_all | solution.py:141
  12.1 0.7 copy-start.4
  13.2 0.9 copy-start.1
  21.8 1.5 %copy-start.5 = (f32[1,128]{1,0:T(1,128)S(1)}, f32[1,128]{1,0:T(1,128)}, u32[]{:S(2)}) copy-start(f32[1,128]{1,0:T(1,128)} %param.18) | copy-start | bytes 1540
  21.8 3.0 %copy-start.3 = (f32[1,128,2]{1,2,0:T(2,128)S(1)}, f32[1,128,2]{1,2,0:T(2,128)}, u32[]{:S(2)}) copy-start(f32[1,128,2]{1,2,0:T(2,128)} %param.14) | copy-start | bytes 3076
  21.8 3.6 %copy-start.6 = (s32[1,128]{1,0:T(1,128)S(1)}, s32[1,128]{1,0:T(1,128)}, u32[]{:S(2)}) copy-start(s32[1,128]{1,0:T(1,128)} %param.15) | copy-start | bytes 1540
  70.0 28.5 %copy-start.2 = (bf16[64,32]{0,1:T(8,128)(2,1)S(1)}, bf16[64,32]{0,1:T(8,128)(2,1)}, u32[]{:S(2)}) copy-start(bf16[64,32]{0,1:T(8,128)(2,1)} %param.21) | copy-start | bytes 12292
  70.0 18.0 %all-to-all-start.2 = ((bf16[16,2,6,2,512]{4,3,2,1,0:T(2,128)(2,1)}), bf16[16,2,6,2,512]{4,3,2,1,0:T(2,128)(2,1)S(1)}, u32[]{:S(2)}, u32[]{:S(2)}) async-start(bf16[16,2,6,2,512]{4,3,2,1,0:T(2,128)(2,1)} %reshape.458), calls=%async_computation.2 | async-start | bytes 786432 | tf_op jit(solution)/shard_map/all_to_all | solution.py:134
  88.1 7.0 %all-to-all-start.1 = ((s32[16,2,6]{0,2,1:T(8,128)}), s32[16,2,6]{0,2,1:T(8,128)S(1)}, u32[]{:S(2)}, u32[]{:S(2)}) async-start(s32[16,2,6]{0,2,1:T(8,128)} %copy.62), calls=%async_computation.1 | async-start | bytes 16384 | tf_op jit(solution)/shard_map/all_to_all | solution.py:140
  95.1 9.4 %all-to-all-start.3 = ((bf16[16,2,6,2,512]{4,3,2,0,1:T(2,128)(2,1)}), bf16[16,2,6,2,512]{4,3,2,0,1:T(2,128)(2,1)S(1)}, u32[]{:S(2)}, u32[]{:S(2)}) async-start(bf16[16,2,6,2,512]{4,3,2,0,1:T(2,128)(2,1)} %copy.68), calls=%async_computation.3 | async-start | bytes 786432 | tf_op jit(solution)/shard_map/all_to_all | solution.py:133
where the time goes:
time: 106 us
  local copies, waits for them, and re-layouts  31.5 us (30%)
  other arithmetic  23.3 us (22%)
  starting transfers between devices  19.9 us (19%)
  waiting for transfers between devices  19.8 us (19%)
  blocking collectives  6.46 us (6%)
  matrix products  3.38 us (3%)
    select_n x18, other arithmetic, cut_windows(): paired = jnp.where(chosen, moved, paired)  16.4 us
    slice x18, local copies, waits for them, and re-layouts, cut_windows(): paired[..., step_size:]  15.4 us
    all_to_all x1, waiting for transfers between devices, on_device(): lax.all_to_all(outgoing, 'pulse', split_axis=0, concat_axis=0, tiled=True)  11.5 us
    all_to_all x1, starting transfers between devices, on_device(): lax.all_to_all(row_slots, 'pulse', split_axis=0, concat_axis=0, tiled=True)  7.39 us
    all_gather x1, blocking collectives, on_device(): raw_echo = lax.all_gather(echo, 'range', axis=2, tiled=True)  6.46 us
    all_to_all x1, starting transfers between devices, on_device(): lax.all_to_all(outgoing, 'pulse', split_axis=0, concat_axis=0, tiled=True)  5.84 us
    all_to_all x1, waiting for transfers between devices, on_device(): lax.all_to_all(lax.all_to_all(outgoing, 'pulse', split_axis=0, concat_axi...  5.52 us
    all_to_all x1, starting transfers between devices, on_device(): lax.all_to_all(lax.all_to_all(outgoing, 'pulse', split_axis=0, concat_axi...  3.47 us
  transfers between devices with their start and end apart: 4, of which 3 were waited for; matrix products, arithmetic and copies ran while one was open for 50% of the time, Pallas kernels for 0%

commit v1 on v0

v1 whole, which is shorter than its diff:
```python
import jax
import jax.numpy as jnp
from jax import lax
from jax.experimental import pallas as pl
from jax.experimental.pallas import tpu as pltpu
from jax.sharding import PartitionSpec as P

SEG = 512
LANE = 128
GROUP = 8
SPAN = SEG + LANE


def chirp_matrix(chirp_phase):
    tap_count = chirp_phase.shape[0]
    tap_scale = 1.0 / jnp.sqrt(jnp.float32(tap_count))
    real_taps = jnp.cos(chirp_phase) * tap_scale
    imag_taps = jnp.sin(chirp_phase) * tap_scale

    def banded(values):
        padded = jnp.concatenate([values, jnp.zeros((tap_count + 1,), jnp.float32)])
        return (
            jnp.tile(padded, tap_count)[: 2 * tap_count * tap_count]
            .reshape(tap_count, 2 * tap_count)
            .T
        )

    real_band = banded(real_taps)
    imag_band = banded(imag_taps)
    upper = jnp.concatenate([real_band, -imag_band], axis=1)
    lower = jnp.concatenate([imag_band, real_band], axis=1)
    return jnp.concatenate([upper, lower], axis=0).astype(jnp.bfloat16)


def compress(echo_block, tail_rim, filter_matrix):
    pulses, planes, bin_count = echo_block.shape
    tap_count = filter_matrix.shape[1] // 2
    block_count = bin_count // tap_count
    extended = jnp.concatenate([echo_block, tail_rim], axis=2)
    left_half = extended[:, :, :bin_count].reshape(pulses, planes, block_count, tap_count)
    right_half = extended[:, :, tap_count:].reshape(pulses, planes, block_count, tap_count)
    windows = jnp.concatenate([left_half, right_half], axis=3)
    windows = windows.transpose(0, 2, 1, 3).reshape(pulses * block_count, 2 * planes * tap_count)
    filtered = jnp.dot(windows, filter_matrix, preferred_element_type=jnp.float32)
    filtered = filtered.reshape(pulses, block_count, planes, tap_count).transpose(0, 2, 1, 3)
    return filtered.reshape(pulses, planes, bin_count).astype(jnp.bfloat16)


def records_kernel(starts_ref, prof_ref, coef_ref, off_ref, out_ref, buf):
    bins = prof_ref.shape[1]
    last_base = bins - SPAN
    groups = out_ref.shape[0] // GROUP

    def group(g, carry):
        for r in range(GROUP):
            st = starts_ref[g * GROUP + r]
            base = pl.multiple_of(jnp.minimum((st // LANE) * LANE, last_base), LANE)
            for kp in range(4):
                buf[kp, pl.ds(r, 1), :] = prof_ref[pl.ds(kp, 1), pl.ds(base, SPAN)]
        rows = pl.ds(pl.multiple_of(g * GROUP, GROUP), GROUP)
        coef = coef_ref[rows, :]
        c0, s0, c1, s1, sc = (coef[:, i : i + 1] for i in range(5))
        re0, im0, re1, im1 = buf[0], buf[1], buf[2], buf[3]
        out_re = ((c0 * re0 + c1 * re1) - (s0 * im0 + s1 * im1)) * sc
        out_im = ((c0 * im0 + c1 * im1) + (s0 * re0 + s1 * re1)) * sc
        off = off_ref[rows, :][:, 0:1]
        for bit in range(8):
            step = 1 << bit
            chosen = ((off >> bit) & 1) == 1
            out_re = jnp.where(chosen, pltpu.roll(out_re, SPAN - step, 1), out_re)
            out_im = jnp.where(chosen, pltpu.roll(out_im, SPAN - step, 1), out_im)
        out_ref[rows, 0:SEG] = out_re[:, :SEG].astype(out_ref.dtype)
        out_ref[rows, SEG : 2 * SEG] = out_im[:, :SEG].astype(out_ref.dtype)
        return carry

    lax.fori_loop(0, groups, group, 0)


def form_records(prof4, starts, coef, offs):
    slots = starts.shape[0]
    vmem = pl.BlockSpec(memory_space=pltpu.VMEM)
    return pl.pallas_call(
        records_kernel,
        out_shape=jax.ShapeDtypeStruct((slots, 2 * SEG), jnp.bfloat16),
        in_specs=[pl.BlockSpec(memory_space=pltpu.SMEM), vmem, vmem, vmem],
        out_specs=vmem,
        scratch_shapes=[pltpu.VMEM((4, GROUP, SPAN), jnp.float32)],
    )(starts, prof4, coef, offs)


def on_device(
    echo,
    chirp_phase,
    rec_phase,
    rec_start,
    rec_owner,
    rec_row,
    rec_weight,
    rec_count,
    prior,
    interp_weight,
):
    pulse_count = lax.axis_size("pulse")
    range_count = lax.axis_size("range")
    owner_total = pulse_count * range_count
    axes = ("pulse", "range")
    me = lax.axis_index("pulse") * range_count + lax.axis_index("range")

    slot_count = rec_start.shape[1]
    owners = rec_owner[0, :, 0]
    dest_rows = rec_row[0]
    out_rows = interp_weight.shape[0]
    capacity = max(2, 3 * slot_count // (2 * owner_total))

    codes = owners * out_rows + dest_rows
    all_codes = lax.all_gather(codes, axes, axis=0, tiled=False)

    filter_matrix = chirp_matrix(chirp_phase)
    tap_count = chirp_phase.shape[0]
    raw_echo = lax.all_gather(echo, "range", axis=2, tiled=True)
    profiles = compress(raw_echo, jnp.zeros_like(raw_echo[:, :, :tap_count]), filter_matrix)
    pulses, planes, bin_total = profiles.shape
    prof4 = profiles.reshape(pulses * planes, bin_total).astype(jnp.float32)

    starts = rec_start[0]
    phases = rec_phase[0]
    weights = rec_weight[0]
    live_mask = (jnp.arange(slot_count) < rec_count[0, 0]).astype(jnp.float32)
    scales = live_mask * weights / jnp.sqrt(jnp.float32(pulses))
    cosine = jnp.cos(phases).astype(jnp.bfloat16).astype(jnp.float32)
    sine_part = jnp.sin(phases).astype(jnp.bfloat16).astype(jnp.float32)
    coef = jnp.stack(
        [cosine[:, 0], sine_part[:, 0], cosine[:, 1], sine_part[:, 1], scales]
        + [jnp.zeros_like(scales)] * 3,
        axis=1,
    )
    base = jnp.minimum(starts // LANE * LANE, bin_total - SPAN)
    offs = jnp.broadcast_to((starts - base)[:, None], (slot_count, LANE)).astype(jnp.int32)
    records = form_records(prof4, starts, coef, offs)

    owner_marks = (owners[:, None] == jnp.arange(owner_total)[None, :]).astype(jnp.int32)
    earlier = jnp.cumsum(owner_marks, axis=0) - owner_marks
    slot_rank = jnp.sum(earlier * owner_marks, axis=1)
    slot_index = owners * capacity + slot_rank
    placement = slot_index[None, :] == jnp.arange(owner_total * capacity)[:, None]
    outgoing = jnp.dot(
        placement.astype(jnp.bfloat16), records, preferred_element_type=jnp.float32
    ).astype(jnp.bfloat16)
    incoming = lax.all_to_all(outgoing, axes, 0, 0, tiled=True)

    mine = (all_codes // out_rows == me).astype(jnp.int32)
    rank = jnp.cumsum(mine, axis=1) - mine
    row_of = all_codes % out_rows
    picks = (mine[:, None, :] == 1) & (rank[:, None, :] == jnp.arange(capacity)[None, :, None])
    slot_rows = jnp.sum(jnp.where(picks, row_of[:, None, :], 0), axis=2).reshape(-1)
    row_table = (slot_rows[None, :] == jnp.arange(out_rows)[:, None]).astype(jnp.bfloat16)

    prior_rows = prior.shape[0]
    fine = jnp.dot(
        interp_weight, prior.reshape(prior_rows, -1), preferred_element_type=jnp.float32
    )
    merged = fine + jnp.dot(row_table, incoming, preferred_element_type=jnp.float32)
    return merged.reshape(out_rows, planes, -1)


def solution(mesh):
    placed = (
        P("pulse", None, "range"),
        P(),
        P("range", "pulse", None),
        P("range", "pulse"),
        P("range", "pulse", None),
        P("range", "pulse"),
        P("range", "pulse"),
        P("range", "pulse"),
        P("pulse", None, "range"),
        P(),
    )
    return jax.shard_map(
        on_device, mesh=mesh, in_specs=placed, out_specs=P("pulse", None, "range"), check_vma=False
    )
```

time: 106 us -> 109 us (1.028)
  blocking collectives: 6.46 us -> 77.9 us
  local copies, waits for them, and re-layouts: 31.5 us -> 7.27 us
  other arithmetic: 23.3 us -> 2.36 us
  waiting for transfers between devices: 19.8 us -> 0.01 us
  starting transfers between devices: 19.9 us -> 6.08 us
  Pallas kernels: 0 us -> 11.4 us
  matrix products: 3.38 us -> 2.12 us
    all_gather x0 -> x1, blocking collectives: none -> 70.8 us  [on_device(): all_codes = lax.all_gather(codes, axes, axis=0, tiled=False)]
    all_to_all x4 -> x1, waiting for transfers between devices: 19.8 us -> 0.01 us  [on_device(): incoming = lax.all_to_all(outgoing, axes, 0, 0, tiled=True)]
    select_n x22 -> x1, other arithmetic: 16.4 us -> 0.01 us  [on_device(): row_of = all_codes % out_rows]
    slice x24 -> x1, local copies, waits for them, and re-layouts: 16.3 us -> 0.01 us  [on_device(): sine_part[:, 1]]
    all_to_all x4 -> x1, starting transfers between devices: 19.9 us -> 6.08 us  [on_device(): incoming = lax.all_to_all(outgoing, axes, 0, 0, tiled=True)]
    pallas_call x0 -> x1, Pallas kernels: none -> 11.4 us  [form_records(): pl.pallas_call(records_kernel, out_shape=jax.ShapeDtypeStruct((slots, 2 *...]
    gather x4 -> x0, local copies, waits for them, and re-layouts: 4.36 us -> none  [the longest x2 2.18 us: cut_windows(): block_table[second_block]]
    dot_general x10 -> x2, matrix products: 2.59 us -> 0.39 us  [the longest x1 0.2 us: on_device(): jnp.dot(interp_weight, prior.reshape(prior_rows, -1), preferred_element_t...]
  transfers between devices with their start and end apart: 4 -> 1, of which waited for: 3 -> 0; matrix products, arithmetic and copies ran while one was open for 50% -> 1% of each run, Pallas kernels for 0% -> 0%
where the time goes in v1:
time: 109 us; the launch traced here: 108 us
  blocking collectives  77.9 us (71%)
  Pallas kernels  11.4 us (10%)
  local copies, waits for them, and re-layouts  7.27 us (7%)
  starting transfers between devices  6.08 us (6%)
  other arithmetic  2.36 us (2%)
  matrix products  2.12 us (2%)
    all_gather x1, blocking collectives, on_device(): all_codes = lax.all_gather(codes, axes, axis=0, tiled=False)  70.8 us
    pallas_call x1, Pallas kernels, form_records(): pl.pallas_call(records_kernel, out_shape=jax.ShapeDtypeStruct((slots, 2 *...  11.4 us
    all_gather x1, blocking collectives, on_device(): raw_echo = lax.all_gather(echo, 'range', axis=2, tiled=True)  7.14 us
    all_to_all x1, starting transfers between devices, on_device(): incoming = lax.all_to_all(outgoing, axes, 0, 0, tiled=True)  6.08 us
  transfers between devices with their start and end apart: 1, of which 0 were waited for; matrix products, arithmetic and copies ran while one was open for 1% of the time, Pallas kernels for 0%

profile of v1, /device:TPU:0, one launch (start us, length us, event | category | flops | bytes accessed | tf_op | source)
XLA Modules:
  0.0 108.2 jit_solution(3600213214792906983)
XLA Ops:
  0.0 0.7 sine_multiply_fusion
  0.8 0.5 tile.21
  1.4 0.1 copy-done.5
  2.3 0.7 copy.29.coef_ref
  3.0 0.2 reshape.133
  3.2 0.2 reshape.132
  3.4 0.6 tile.9
  4.1 0.2 reshape.130
  4.3 7.1 %all_gather.8 = bf16[2,2,32768]{2,1,0:T(2,128)(2,1)S(1)} all-gather(bf16[2,2,16384]{2,1,0:T(2,128)(2,1)S(1)} %copy-done.1), channel_id=1, replica_groups=mesh['pulse'=16,'range'=2] {'range'}, dimensions={2}, use_global_device_ids=true | all-gather | bytes 393216 | tf_op jit(solution)/shard_map/all_gather | solution.py:120
  11.4 0.2 pad_slice_fusion
  11.7 0.5 maximum_bitcast_fusion
  12.1 0.4 reshape.136
  12.5 0.1 maximum_maximum_fusion
  12.6 0.5 fusion
  13.2 1.1 %copy.32 = f32[1,4,128,256]{3,1,2,0:T(4,128)} copy(f32[1,4,128,256]{3,2,1,0:T(8,128)S(1)} %bitcast.54) | data formatting | bytes 1048576
  14.3 0.1 fusion.3
  14.4 0.2 reduce_window_sum.23
  14.6 0.2 select_reduce_fusion.1
  14.8 0.7 broadcast_in_dim.12.off_ref
  15.5 11.4 %shard_map.100 = bf16[128,1024]{1,0:T(8,128)(2,1)} custom-call(s32[128]{0:T(128)} %bitcast.65, f32[4,32768]{1,0:T(4,128)} %bitcast.53, f32[128,8]{1,0:T(8,128)} %copy.29.coef_ref, s32[128,128]{1,0:T(8,128)} %broadcast_in_dim.12.off_ref), custom_call_target="tpu_custom_call" | custom-call | tf_op jit(solution)/shard_map/pallas_call | solution.py:82
  26.9 1.2 %convolution_convert_fusion = bf16[192,1024]{1,0:T(8,128)(2,1)S(1)} fusion(bf16[128,1024]{1,0:T(8,128)(2,1)} %shard_map.100, s32[128]{0:T(128)S(1)} %multiply_add_fusion), kind=kOutput, calls=%fused_computation | convolution fusion | flops 50552832 | bytes 655872 | tf_op jit(solution)/shard_map/dot_general | solution.py:146
  28.2 0.9 all_to_all.8
  29.1 6.1 %all-to-all-start = ((bf16[32,6,1024]{2,1,0:T(8,128)(2,1)}), bf16[32,6,1024]{2,1,0:T(8,128)(2,1)S(1)}, u32[]{:S(2)}, u32[]{:S(2)}) async-start(bf16[32,6,1024]{2,1,0:T(8,128)(2,1)} %all_to_all.8), calls=%async_computation | async-start | bytes 1048576 | tf_op jit(solution)/shard_map/all_to_all | solution.py:149
  35.2 70.8 %all-gather = s32[32,1,128]{2,1,0:T(1,128)S(1)} all-gather(s32[1,1,128]{2,1,0:T(1,128)S(1)} %fusion.15), channel_id=1, replica_groups=mesh['pulse'=16,'range'=2] {'pulse','range'}, dimensions={0}, use_global_device_ids=true | all-gather | bytes 16896 | tf_op jit(solution)/shard_map/all_gather | solution.py:116
  106.0 0.3 reduce_window_sum.22
  106.3 0.2 select_reduce_fusion
  106.5 0.1 copy.26
  106.6 0.1 eq.73
  106.7 0.2 fusion.19
  106.9 0.1 all_to_all.10
  107.1 0.2 convolution_add_fusion
  107.3 0.9 reshape.126
  (39 shorter events, 0.5 us)
Async XLA Ops:
  0.0 106.7 %copy-start = (bf16[64,32]{0,1:T(8,128)(2,1)S(1)}, bf16[64,32]{0,1:T(8,128)(2,1)}, u32[]{:S(2)}) copy-start(bf16[64,32]{0,1:T(8,128)(2,1)} %param.19) | copy-start | bytes 12292
  0.8 0.7 copy-start.5
  0.8 0.7 copy-start.4
  0.8 1.4 %copy-start.7 = (f32[1,128]{1,0:T(1,128)S(1)}, f32[1,128]{1,0:T(1,128)}, u32[]{:S(2)}) copy-start(f32[1,128]{1,0:T(1,128)} %param.16) | copy-start | bytes 1540
  3.4 0.9 copy-start.1
  13.1 1.2 %copy-start.6 = (s32[1,128]{1,0:T(1,128)S(1)}, s32[1,128]{1,0:T(1,128)}, u32[]{:S(2)}) copy-start(s32[1,128]{1,0:T(1,128)} %param.13) | copy-start | bytes 1540
  13.2 1.2 %copy-start.3 = (s32[1,128,1]{1,2,0:T(1,128)S(1)}, s32[1,128,1]{1,2,0:T(1,128)}, u32[]{:S(2)}) copy-start(s32[1,128,1]{1,2,0:T(1,128)} %param.14) | copy-start | bytes 1540
  28.1 7.0 %copy-start.8 = (s32[1,128]{1,0:T(1,128)S(1)}, s32[1,128]{1,0:T(1,128)}, u32[]{:S(2)}) copy-start(s32[1,128]{1,0:T(1,128)} %param.15) | copy-start | bytes 1540
  28.1 78.5 %copy-start.2 = (bf16[32,2,512]{2,1,0:T(2,128)(2,1)S(1)}, bf16[32,2,512]{2,1,0:T(2,128)(2,1)}, u32[]{:S(2)}) copy-start(bf16[32,2,512]{2,1,0:T(2,128)(2,1)} %param.18) | copy-start | bytes 196612
  29.1 77.8 %all-to-all-start = ((bf16[32,6,1024]{2,1,0:T(8,128)(2,1)}), bf16[32,6,1024]{2,1,0:T(8,128)(2,1)S(1)}, u32[]{:S(2)}, u32[]{:S(2)}) async-start(bf16[32,6,1024]{2,1,0:T(8,128)(2,1)} %all_to_all.8), calls=%async_computation | async-start | bytes 1048576 | tf_op jit(solution)/shard_map/all_to_all | solution.py:149
